TPU v7x, 128 devices: a whole 4x4x4 slice. The times are simulated.
128 devices in a mesh: row: 8 (over x, core), col: 16 (over y, z).
Axes of the slice: x: 4, y: 4, z: 4, core: 2. Of those that a mesh axis runs over, the one named last changes fastest.
Arguments:
- front_matrix: float32 [16384, 16384], P('row', 'col'), may hold values from -2.5 to 202.5, as said below
- child_schur: float32 [2, 8192, 8192], P(None, 'row', 'col'), may hold values from -1.25 to 1.25
- child_index: int32 [2, 128], replicated, may hold values from 0 to 255, as said below
- child_valid: int32 [2, 128], replicated, may hold values 0 or 1
Outputs:
- trailing: float32 [16384, 16384], P('row', 'col')
- panel_factor: float32 [16384, 512], P('row')
Inputs may be any that keep to these rules, and one draw needn't show every extreme that they name: `front_matrix`: off the logical diagonal the entries lie in -2.5 to 2.5, on it in 97.5 to 202.5. `child_index`: each child's 128 entries are distinct front blocks. Among the child blocks a that share a mod 8, exactly 2 land in front blocks of each value mod 8; among the child blocks b that share b mod 16, at most 1 land in front blocks of any one value mod 16, and some value takes exactly 1.
All inputs are finite; a program needn't handle non-finite values.
Results may differ from a plain program's by a relative error of at most 0.00005.
Values sent between devices are 32-bit elements; how exact they have to be, the bound alone decides.
No kernel may reach another device: no remote copies, remote signals or barrier semaphores. Data moves between devices by JAX's collectives and lax.ppermute only.
A program may use at most 256 MiB of HBM per device.

v0:
```python
import jax
import jax.numpy as jnp
from jax import lax
from jax.sharding import PartitionSpec as P

CHILD = 8192
PANEL = 512
BLK = 64
exact_mode = lax.Precision.HIGHEST


def take_slabs(source, indices):
    return jnp.take(source, indices, axis=0)


def on_device(front_matrix, child_schur, child_index, child_valid):
    row_count = lax.axis_size("row")
    col_count = lax.axis_size("col")
    row_place = lax.axis_index("row")
    col_place = lax.axis_index("col")
    local_rows, local_cols = front_matrix.shape
    row_blocks = local_rows // BLK
    col_blocks = local_cols // BLK
    child_blocks = CHILD // BLK
    child_rowblk = child_schur.shape[1] // BLK
    child_colblk = child_schur.shape[2] // BLK
    per_owner = child_blocks // (row_count * row_count)
    col_multi = max(1, child_blocks // (col_count * col_count))
    row_slots = row_count * per_owner
    col_slots = col_count * col_multi
    validity = child_valid.astype(jnp.float32)
    all_blocks = jnp.arange(child_blocks)
    owner_row = child_index % row_count
    owner_col = child_index % col_count
    sender_row = all_blocks % row_count
    sender_col = all_blocks % col_count
    before = all_blocks[None, :] < all_blocks[:, None]
    earlier_row = (sender_row[:, None] == sender_row[None, :]) & before
    earlier_col = (sender_col[:, None] == sender_col[None, :]) & before
    row_rank = jnp.sum(
        (earlier_row[None] & (owner_row[:, :, None] == owner_row[:, None, :])).astype(jnp.int32),
        axis=2,
    )
    col_rank = jnp.sum(
        (earlier_col[None] & (owner_col[:, :, None] == owner_col[:, None, :])).astype(jnp.int32),
        axis=2,
    )
    row_key = owner_row * per_owner + row_rank
    col_key = owner_col * col_multi + col_rank
    local_arow = row_place + row_count * jnp.arange(child_rowblk)
    mine_rowkey = jnp.take(row_key, local_arow, axis=1)
    row_hit_send = mine_rowkey[:, :, None] == jnp.arange(row_slots)[None, None, :]
    src_row = jnp.sum(
        row_hit_send.astype(jnp.int32) * jnp.arange(child_rowblk)[None, :, None], axis=1
    )
    local_bcol = col_place + col_count * jnp.arange(child_colblk)
    mine_colkey = jnp.take(col_key, local_bcol, axis=1)
    col_hit_send = mine_colkey[:, :, None] == jnp.arange(col_slots)[None, None, :]
    src_col = jnp.sum(
        col_hit_send.astype(jnp.int32) * jnp.arange(child_colblk)[None, :, None], axis=1
    )
    has_col = jnp.sum(col_hit_send.astype(jnp.float32), axis=1)
    blocks = child_schur.reshape(2, child_rowblk, BLK, child_colblk * BLK)
    outgoing = jax.vmap(take_slabs)(blocks, src_row)
    outgoing = outgoing.reshape(2, row_slots * BLK, child_colblk * BLK)
    section_one = lax.all_to_all(outgoing, "row", split_axis=1, concat_axis=1, tiled=True)
    flipped = jnp.swapaxes(section_one, 1, 2).reshape(2, child_colblk, BLK, row_slots * BLK)
    onward = jax.vmap(take_slabs)(flipped, src_col) * has_col[:, :, None, None]
    onward = onward.reshape(2, col_slots * BLK, row_slots * BLK)
    section_two = lax.all_to_all(onward, "col", split_axis=1, concat_axis=1, tiled=True)
    arrived = section_two.reshape(2, col_slots, BLK, row_slots * BLK)
    front_rowblk = row_place + row_count * jnp.arange(row_blocks)
    match_rows = (child_index[:, None, :] == front_rowblk[None, :, None]).astype(jnp.int32)
    row_slot_of = sender_row[None, :] * per_owner + row_rank
    row_source = jnp.sum(match_rows * row_slot_of[:, None, :], axis=2)
    row_weight = jnp.sum(match_rows.astype(jnp.float32) * validity[:, None, :], axis=2)
    front_colblk = col_place + col_count * jnp.arange(col_blocks)
    match_cols = (child_index[:, None, :] == front_colblk[None, :, None]).astype(jnp.int32)
    col_slot_of = sender_col[None, :] * col_multi + col_rank
    col_source = jnp.sum(match_cols * col_slot_of[:, None, :], axis=2)
    col_weight = jnp.sum(match_cols.astype(jnp.float32) * validity[:, None, :], axis=2)
    by_col = jax.vmap(take_slabs)(arrived, col_source) * col_weight[:, :, None, None]
    by_col = by_col.reshape(2, local_cols, row_slots * BLK)
    unflipped = jnp.swapaxes(by_col, 1, 2).reshape(2, row_slots, BLK, local_cols)
    placed = jax.vmap(take_slabs)(unflipped, row_source) * row_weight[:, :, None, None]
    placed = placed.reshape(2, local_rows, local_cols)
    extended = front_matrix + placed[0] + placed[1]
    panel_width = PANEL // BLK
    spread = col_count // panel_width
    lead = extended[:, :BLK]
    lifted = lax.ppermute(
        lead,
        "col",
        [(c, c + panel_width * s) for s in range(1, spread) for c in range(panel_width)],
    )
    mine = jnp.where(col_place < panel_width, lead, lifted)
    part_rows = local_rows // spread
    part = lax.dynamic_slice_in_dim(mine, col_place // panel_width * part_rows, part_rows, axis=0)
    gathered = lax.all_gather(part, "col", axis=0, tiled=False)
    gathered = gathered.reshape(spread, panel_width, part_rows, BLK)
    panel_cols = gathered.transpose(0, 2, 1, 3).reshape(local_rows, PANEL)
    corner = lax.all_gather(panel_cols[: PANEL // row_count], "row", axis=0, tiled=True)
    lower_factor = jnp.linalg.cholesky(corner)
    solved = jax.scipy.linalg.solve_triangular(lower_factor, panel_cols.T, lower=True).T
    logical_blk = jnp.arange(row_blocks) * row_count + row_place
    factor_blocks = lower_factor.reshape(panel_width, BLK, PANEL)
    picked = jnp.take(factor_blocks, jnp.minimum(logical_blk, panel_width - 1), axis=0)
    in_panel = (logical_blk < panel_width)[:, None, None]
    panel_factor = jnp.where(in_panel, picked, solved.reshape(row_blocks, BLK, PANEL)).reshape(
        local_rows, PANEL
    )
    ratio = col_count // row_count
    arranged = panel_factor.reshape(col_blocks, ratio, BLK, PANEL)
    chosen = lax.dynamic_index_in_dim(arranged, col_place // row_count, axis=1, keepdims=False)
    chosen = chosen.reshape(col_blocks * BLK, PANEL)
    pairs = []
    for r0 in range(row_count):
        for c1 in range(col_count):
            dest_row = c1 % row_count
            dest_col = r0 + row_count * (c1 // row_count)
            pairs.append((r0 * col_count + c1, dest_row * col_count + dest_col))
    across = lax.ppermute(chosen, ("row", "col"), pairs)
    update = jnp.einsum("rp,cp->rc", panel_factor, across, precision=exact_mode)
    logical_row = jnp.arange(local_rows) // BLK * row_count + row_place
    logical_col = jnp.arange(local_cols) // BLK * col_count + col_place
    retained = (logical_row >= panel_width)[:, None] & (logical_col >= panel_width)[None, :]
    trailing = jnp.where(retained, extended - update, jnp.zeros_like(update))
    return (trailing, panel_factor)


def solution(mesh):
    in_specs = (P("row", "col"), P(None, "row", "col"), P(), P())
    out_specs = (P("row", "col"), P("row", None))
    return jax.shard_map(
        on_device, mesh=mesh, in_specs=in_specs, out_specs=out_specs, check_vma=False
    )
```

profile of v0, /device:TPU:7, one launch (start us, length us, event | category | flops | bytes accessed | tf_op | source)
XLA Modules:
  0.0 768.0 jit_solution(1678104543497816341)
XLA Ops:
  10.7 5.0 gather_fusion.3
  15.7 2.5 bitcast_select_fusion.2
  18.2 5.2 copy.126
  23.4 5.1 all-to-all-start
  29.0 46.6 %all-to-all-done = f32[2,1024,512]{2,0,1:T(2,128)} async-done(((f32[2,1024,512]{2,0,1:T(2,128)}), f32[2,1024,512]{2,0,1:T(2,128)}, u32[]{:S(2)}, u32[]{:S(2)}) %all-to-all-start) | async-done | bytes 4194336 | tf_op jit(solution)/shard_map/all_to_all | solution.py:66
  75.6 7.2 copy.127
  82.8 6.7 gather_fusion.4
  89.5 3.9 fusion.2
  93.4 12.9 %copy.128 = f32[2,1024,1024]{2,0,1:T(2,128)} copy(f32[2,1024,1024]{2,1,0:T(8,128)S(1)} %fusion.2) | data formatting | bytes 16777216 | tf_op jit(solution)/shard_map/mul | solution.py:68
  106.3 8.1 %all-to-all-start.1 = ((f32[2,1024,1024]{2,0,1:T(2,128)}), f32[2,1024,1024]{2,0,1:T(2,128)}, u32[]{:S(2)}, u32[]{:S(2)}) async-start(f32[2,1024,1024]{2,0,1:T(2,128)} %copy.128), calls=%async_computation.1 | async-start | bytes 16777216 | tf_op jit(solution)/shard_map/all_to_all | solution.py:70
  115.9 140.9 %all-to-all-done.1 = f32[2,1024,1024]{2,0,1:T(2,128)} async-done(((f32[2,1024,1024]{2,0,1:T(2,128)}), f32[2,1024,1024]{2,0,1:T(2,128)}, u32[]{:S(2)}, u32[]{:S(2)}) %all-to-all-start.1) | async-done | bytes 8388640 | tf_op jit(solution)/shard_map/all_to_all | solution.py:70
  256.8 9.5 %copy.129 = f32[2,1024,1024]{2,1,0:T(8,128)} copy(f32[2,1024,1024]{2,0,1:T(2,128)} %all-to-all-done.1) | data formatting | bytes 16777216 | tf_op jit(solution)/shard_map/all_to_all | solution.py:70
  266.3 7.7 %gather_fusion.5 = f32[32,64,1024]{2,1,0:T(8,128)} fusion(f32[2,16,64,1024]{3,2,1,0:T(8,128)} %bitcast.129, s32[32]{0:T(128)S(1)} %reshape.535), kind=kCustom, calls=%fused_computation.5 | custom fusion | bytes 16777472 | tf_op jit(solution)/shard_map/vmap(jit(_take))/gather | solution.py:13
  274.0 6.0 fusion.1
  280.0 8.7 %copy.130 = f32[2,1024,1024]{2,1,0:T(8,128)} copy(f32[2,1024,1024]{1,2,0:T(8,128)} %fusion.1) | data formatting | bytes 16777216 | tf_op jit(solution)/shard_map/transpose | solution.py:84
  288.7 12.5 %gather_fusion.6 = f32[64,64,1024]{2,1,0:T(8,128)} fusion(f32[2,16,64,1024]{3,2,1,0:T(8,128)} %bitcast.124, s32[64]{0:T(128)S(1)} %reshape.541), kind=kCustom, calls=%fused_computation.6 | custom fusion | bytes 33554944 | tf_op jit(solution)/shard_map/vmap(jit(_take))/gather | solution.py:13
  301.2 7.3 select_multiply_fusion
  308.5 6.7 fusion.77
  315.2 9.7 %bitcast_add_fusion = f32[2048,1024]{1,0:T(8,128)S(1)} fusion(f32[1,32,64,1024]{3,2,1,0:T(8,128)} %get-tuple-element.35, f32[2048,1024]{1,0:T(8,128)} %param.4, f32[1,32,64,1024]{3,2,1,0:T(8,128)} %get-tuple-element.34), kind=kLoop, calls=%fused_computation.10 | loop fusion | flops 4194304 | bytes 33554432 | tf_op jit(solution)/shard_map/add | solution.py:87
  325.0 3.4 copy-done
  328.8 1.3 collective-permute-start
  330.2 8.5 %collective-permute-done = f32[2048,64]{0,1:T(8,128)S(1)} collective-permute-done((f32[2048,64]{0,1:T(8,128)S(1)}, f32[2048,64]{0,1:T(8,128)S(1)}, u32[]{:S(2)}, u32[]{:S(2)}) %collective-permute-start) | collective-permute-done | bytes 524320 | tf_op jit(solution)/shard_map/ppermute | solution.py:91
  338.9 0.9 dynamic-slice_select_fusion.2
  339.9 84.5 %all-gather.6.cloned.1.call-done = f32[16384,64]{1,0:T(8,128)} async-done(((f32[1024,64]{1,0:T(8,128)}), f32[16384,64]{1,0:T(8,128)}) %all-gather.6.cloned.1.call-update) | async-done | bytes 4194320 | tf_op jit(solution)/shard_map/all_gather | solution.py:99
  424.4 9.0 %copy.133 = f32[2,8,1024,64]{2,0,3,1:T(2,128)} copy(f32[2,8,1024,64]{3,2,1,0:T(8,128)} %bitcast.141) | data formatting | bytes 8388608 | tf_op jit(solution)/shard_map/reshape | solution.py:100
  433.4 4.1 copy.142
  437.6 2.0 copy-done.1
  439.6 0.8 copy.134
  440.8 21.5 %all-gather.4.cloned.1.call-done = f32[512,512]{1,0:T(8,128)} async-done(((f32[64,512]{1,0:T(8,128)}), f32[512,512]{1,0:T(8,128)}) %all-gather.4.cloned.1.call-update) | async-done | bytes 1048592 | tf_op jit(solution)/shard_map/all_gather | solution.py:102
  462.3 1.6 copy.135
  463.9 1.4 fusion.17
  465.3 11.7 %cholesky.104 = f32[128,128]{1,0:T(8,128)S(1)} custom-call(f32[128,128]{1,0:T(8,128)S(1)} %cholesky.266), custom_call_target="Cholesky" | custom-call | tf_op jit(solution)/shard_map/jit(cholesky)/cholesky | solution.py:103
  477.2 9.8 %custom-call.31 = f32[1,128,128]{1,2,0:T(8,128)S(1)} custom-call(f32[1,128,128]{2,1,0:T(8,128)S(1)} %get-tuple-element.45), custom_call_target="InvertDiagBlocksLowerTriangular" | custom-call | tf_op jit(solution)/shard_map/jit(cholesky)/cholesky | solution.py:103
  487.7 11.9 %cholesky.217 = f32[128,128]{1,0:T(8,128)S(1)} custom-call(f32[128,128]{1,0:T(8,128)S(1)} %cholesky.270), custom_call_target="Cholesky" | custom-call | tf_op jit(solution)/shard_map/jit(cholesky)/cholesky | solution.py:103
  500.2 0.7 compare_reduce_fusion.3
  500.9 9.8 %custom-call.32 = f32[1,128,128]{1,2,0:T(8,128)S(1)} custom-call(f32[1,128,128]{2,1,0:T(8,128)S(1)} %get-tuple-element.42), custom_call_target="InvertDiagBlocksLowerTriangular" | custom-call | tf_op jit(solution)/shard_map/jit(cholesky)/cholesky | solution.py:103
  511.4 11.7 %cholesky.238 = f32[128,128]{1,0:T(8,128)S(1)} custom-call(f32[128,128]{1,0:T(8,128)S(1)} %cholesky.275), custom_call_target="Cholesky" | custom-call | tf_op jit(solution)/shard_map/jit(cholesky)/cholesky | solution.py:103
  523.8 9.8 %custom-call.33 = f32[1,128,128]{1,2,0:T(8,128)S(1)} custom-call(f32[1,128,128]{2,1,0:T(8,128)S(1)} %get-tuple-element.39), custom_call_target="InvertDiagBlocksLowerTriangular" | custom-call | tf_op jit(solution)/shard_map/jit(cholesky)/cholesky | solution.py:103
  534.2 11.9 %cholesky.255 = f32[128,128]{1,0:T(8,128)S(1)} custom-call(f32[128,128]{1,0:T(8,128)S(1)} %convolution_subtract_fusion.4), custom_call_target="Cholesky" | custom-call | tf_op jit(solution)/shard_map/jit(cholesky)/cholesky | solution.py:103
  546.2 0.7 compare_reduce_fusion
  549.7 10.5 %while.1 = (s32[]{:T(128)}, f32[512,512]{1,0:T(8,128)S(1)}, s32[4,2]{0,1:T(2,128)S(1)}, f32[4,128,128]{2,1,0:T(8,128)}, s32[]{:T(128)}) while((s32[]{:T(128)}, f32[512,512]{1,0:T(8,128)S(1)}, s32[4,2]{0,1:T(2,128)S(1)}, f32[4,128,128]{2,1,0:T(8,128)}, s32[]{:T(128)}) %tuple.44), condition=%wide.while_cond, body=%wide.while_body.sunk | while | flops 2 | bytes 132705 | solution.py:104
  550.4 2.0 bitcast_dynamic-update-slice_fusion.2
  553.0 2.0 bitcast_dynamic-update-slice_fusion.2
  555.6 2.0 bitcast_dynamic-update-slice_fusion.2
  558.3 2.0 bitcast_dynamic-update-slice_fusion.2
  560.2 40.2 %custom-call.34 = f32[4,128,128]{1,2,0:T(8,128)S(1)} custom-call(f32[4,128,128]{2,1,0:T(8,128)} %get-tuple-element.9), custom_call_target="InvertDiagBlocksLowerTriangular" | custom-call | tf_op jit(solution)/shard_map/jit(_solve_triangular)/triangular_solve | solution.py:104
  600.4 2.4 fusion.15
  602.8 2.2 convolution_subtract_fusion.1
  605.1 1.1 fusion.30
  606.2 2.2 convolution_subtract_fusion
  608.3 1.1 fusion.28
  609.4 3.2 fusion.9
  612.6 1.0 fusion.27
  613.7 1.1 copy-done.5
  614.7 2.4 maximum_bitcast_fusion
  617.1 5.3 copy.139
  622.5 2.8 gather_fusion.2
  625.3 4.2 dynamic-slice_select_fusion
  629.5 7.2 collective-permute-start.1
  637.1 5.7 copy.136
  642.8 5.4 select_select_fusion
  648.2 5.3 copy.140
  653.5 75.5 %collective-permute-done.1 = f32[1024,512]{1,0:T(8,128)} collective-permute-done((f32[1024,512]{1,0:T(8,128)}, f32[1024,512]{1,0:T(8,128)}, u32[]{:S(2)}, u32[]{:S(2)}) %collective-permute-start.1) | collective-permute-done | bytes 2097184 | tf_op jit(solution)/shard_map/ppermute | solution.py:122
  729.1 31.7 %subtract_select_fusion = f32[2048,1024]{1,0:T(8,128)} fusion(f32[2048,1024]{1,0:T(8,128)} %copy-done, pred[1024]{0:T(1024)(128)(4,1)S(1)} %fusion.54, pred[2048]{0:T(1024)(128)(4,1)S(1)} %fusion.48, f32[2048,512]{0,1:T(8,128)} %select_select_fusion, f32[1024,512]{1,0:T(8,128)} %collective-permute-done.1), kind=kOutput, calls=%fused_computation.17 | convolution fusion | flops 12891193344 | bytes 23071744 | tf_op jit(solution)/shard_map/rp,cp->rc/dot_general | solution.py:123
  (121 shorter events, 13.3 us)
Async XLA Ops:
  23.4 52.2 %all-to-all-start = ((f32[2,1024,512]{2,0,1:T(2,128)}), f32[2,1024,512]{2,0,1:T(2,128)}, u32[]{:S(2)}, u32[]{:S(2)}) async-start(f32[2,1024,512]{2,0,1:T(2,128)} %copy.126), calls=%async_computation | async-start | bytes 8388608 | tf_op jit(solution)/shard_map/all_to_all | solution.py:66
  106.3 8.3 %copy-start.7 = (s32[2,128]{1,0:T(2,128)S(1)}, s32[2,128]{1,0:T(2,128)}, u32[]{:S(2)}) copy-start(s32[2,128]{1,0:T(2,128)} %param.6) | copy-start | bytes 3076
  106.3 8.8 %copy-start.8 = (s32[2,128]{1,0:T(2,128)S(1)}, s32[2,128]{1,0:T(2,128)}, u32[]{:S(2)}) copy-start(s32[2,128]{1,0:T(2,128)} %param.7) | copy-start | bytes 3076
  106.3 150.5 %all-to-all-start.1 = ((f32[2,1024,1024]{2,0,1:T(2,128)}), f32[2,1024,1024]{2,0,1:T(2,128)}, u32[]{:S(2)}, u32[]{:S(2)}) async-start(f32[2,1024,1024]{2,0,1:T(2,128)} %copy.128), calls=%async_computation.1 | async-start | bytes 16777216 | tf_op jit(solution)/shard_map/all_to_all | solution.py:70
  114.4 310.0 %all-gather.6.cloned.1.call-start = ((), (), s32[]{:S(2)}) async-start(), calls=%async_computation.3 | async-start | bytes 8912896 | tf_op jit(solution)/shard_map/all_gather | solution.py:99
  325.0 3.4 copy-start
  328.8 9.9 %collective-permute-start = (f32[2048,64]{0,1:T(8,128)S(1)}, f32[2048,64]{0,1:T(8,128)S(1)}, u32[]{:S(2)}, u32[]{:S(2)}) collective-permute-start(f32[2048,64]{0,1:T(8,128)S(1)} %copy.131), channel_id=1, source_target_pairs={{0,8},{1,9},{2,10},{3,11},{4,12},{5,13},{6,14},{7,15},{16,24},{17,... | collective-permute-start | bytes 1572872 | tf_op jit(solution)/shard_map/ppermute | solution.py:91
  339.8 122.5 %all-gather.4.cloned.1.call-start = ((), (), s32[]{:S(2)}) async-start(), calls=%async_computation.2 | async-start | bytes 1179648 | tf_op jit(solution)/shard_map/all_gather | solution.py:102
  437.6 2.0 copy-start.1
  560.2 42.6 %copy-start.6 = (f32[512,512]{1,0:T(8,128)}, f32[512,512]{1,0:T(8,128)S(1)}, u32[]{:S(2)}) copy-start(f32[512,512]{1,0:T(8,128)S(1)} %get-tuple-element.112) | copy-start | bytes 3145732
  600.4 5.7 copy-start.2
  609.4 4.2 copy-start.3
  613.7 1.1 copy-start.5
  629.5 99.5 %collective-permute-start.1 = (f32[1024,512]{1,0:T(8,128)}, f32[1024,512]{1,0:T(8,128)}, u32[]{:S(2)}, u32[]{:S(2)}) collective-permute-start(f32[1024,512]{1,0:T(8,128)} %bitcast.40), channel_id=1, source_target_pairs={{0,0},{1,16},{2,32},{3,48},{4,64},{5,80},{6,96},{7,112},{8,8},{9,2... | collective-permute-start | bytes 6291464 | tf_op jit(solution)/shard_map/ppermute | solution.py:122
  637.1 5.7 copy-start.4
Sparse Core Ops, SparseCore 0:
  339.9 84.4 all-gather.5
  440.5 21.7 all-gather.3
where the time goes:
time: 777 us; the launch traced here: 768 us
  waiting for transfers between devices  378 us (49%)
  other arithmetic  166 us (21%)
  local copies, waits for them, and re-layouts  138 us (18%)
  matrix products  46.7 us (6%)
  starting transfers between devices  22 us (3%)
  between operations  17.6 us (2%)
    all_to_all x1, waiting for transfers between devices, on_device(): lax.all_to_all(onward, 'col', split_axis=1, concat_axis=1, tiled=True)  141 us
    all_gather x1, waiting for transfers between devices, on_device(): gathered = lax.all_gather(part, 'col', axis=0, tiled=False)  84.5 us
    another operation x15, other arithmetic, on_device(): lower_factor = jnp.linalg.cholesky(corner)  79.5 us
    ppermute x1, waiting for transfers between devices, on_device(): across = lax.ppermute(chosen, ('row', 'col'), pairs)  75.5 us
    all_to_all x1, waiting for transfers between devices, on_device(): lax.all_to_all(outgoing, 'row', split_axis=1, concat_axis=1, tiled=True)  46.6 us
    another operation x3, other arithmetic, on_device(): jax.scipy.linalg.solve_triangular(lower_factor, panel_cols.T, lower=True)  40.4 us
    gather x8, local copies, waits for them, and re-layouts, take_slabs(): return jnp.take(source, indices, axis=0)  32.2 us
    dot_general x1, matrix products, on_device(): update = jnp.einsum('rp,cp->rc', panel_factor, across, precision=exact_mode)  31.7 us
  transfers between devices with their start and end apart: 6, of which 6 were waited for; matrix products, arithmetic and copies ran while one was open for 2% of the time, Pallas kernels for 0%

commit v1 on v0

--- a/solution.py
+++ b/solution.py
@@ -99,7 +99,15 @@
     gathered = lax.all_gather(part, "col", axis=0, tiled=False)
     gathered = gathered.reshape(spread, panel_width, part_rows, BLK)
     panel_cols = gathered.transpose(0, 2, 1, 3).reshape(local_rows, PANEL)
-    corner = lax.all_gather(panel_cols[: PANEL // row_count], "row", axis=0, tiled=True)
+    corner = jnp.concatenate(
+        lax.all_to_all(
+            jnp.stack(lax.psum(1, axis_name="row") * [panel_cols[: PANEL // row_count]], 0),
+            axis_name="row",
+            split_axis=0,
+            concat_axis=0,
+        ),
+        axis=0,
+    )
     lower_factor = jnp.linalg.cholesky(corner)
     solved = jax.scipy.linalg.solve_triangular(lower_factor, panel_cols.T, lower=True).T
     logical_blk = jnp.arange(row_blocks) * row_count + row_place

time: 777 us -> 771 us (level)
  waiting for transfers between devices: 378 us -> 369 us
    all_gather x1 -> x0, waiting for transfers between devices: 21.5 us -> none  [on_device(): lax.all_gather(panel_cols[:PANEL // row_count], 'row', axis=0, tiled=True)]
    all_to_all x0 -> x1, waiting for transfers between devices: none -> 12.4 us  [on_device(): lax.all_to_all(jnp.stack(lax.psum(1, axis_name='row') * [panel_cols[:PANE...]
where the time goes in v1:
time: 771 us; the launch traced here: 762 us
  waiting for transfers between devices  369 us (48%)
  other arithmetic  165 us (21%)
  local copies, waits for them, and re-layouts  137 us (18%)
  matrix products  46.7 us (6%)
  starting transfers between devices  26.8 us (3%)
  between operations  17.8 us (2%)
    all_to_all x1, waiting for transfers between devices, on_device(): lax.all_to_all(onward, 'col', split_axis=1, concat_axis=1, tiled=True)  141 us
    all_gather x1, waiting for transfers between devices, on_device(): gathered = lax.all_gather(part, 'col', axis=0, tiled=False)  84.6 us
    another operation x15, other arithmetic, on_device(): lower_factor = jnp.linalg.cholesky(corner)  79.3 us
    ppermute x1, waiting for transfers between devices, on_device(): across = lax.ppermute(chosen, ('row', 'col'), pairs)  76.4 us
    all_to_all x1, waiting for transfers between devices, on_device(): lax.all_to_all(outgoing, 'row', split_axis=1, concat_axis=1, tiled=True)  46.6 us
    another operation x3, other arithmetic, on_device(): jax.scipy.linalg.solve_triangular(lower_factor, panel_cols.T, lower=True)  40.4 us
    gather x8, local copies, waits for them, and re-layouts, take_slabs(): return jnp.take(source, indices, axis=0)  32.2 us
    dot_general x1, matrix products, on_device(): update = jnp.einsum('rp,cp->rc', panel_factor, across, precision=exact_mode)  31.7 us
  transfers between devices with their start and end apart: 6, of which 6 were waited for; matrix products, arithmetic and copies ran while one was open for 2% of the time, Pallas kernels for 0%

profile of v1, /device:TPU:7, one launch (start us, length us, event | category | flops | bytes accessed | tf_op | source)
XLA Modules:
  0.0 762.4 jit_solution(14622390053163177061)
XLA Ops:
  7.3 0.7 and_select_fusion
  10.7 5.0 gather_fusion.3
  15.7 2.5 bitcast_select_fusion.2
  18.2 5.2 copy.127
  23.4 5.1 all-to-all-start
  29.0 46.6 %all-to-all-done = f32[2,1024,512]{2,0,1:T(2,128)} async-done(((f32[2,1024,512]{2,0,1:T(2,128)}), f32[2,1024,512]{2,0,1:T(2,128)}, u32[]{:S(2)}, u32[]{:S(2)}) %all-to-all-start) | async-done | bytes 4194336 | tf_op jit(solution)/shard_map/all_to_all | solution.py:66
  75.6 7.2 copy.128
  82.8 6.7 gather_fusion.4
  89.5 3.9 fusion.2
  93.4 12.9 %copy.129 = f32[2,1024,1024]{2,0,1:T(2,128)} copy(f32[2,1024,1024]{2,1,0:T(8,128)S(1)} %fusion.2) | data formatting | bytes 16777216 | tf_op jit(solution)/shard_map/mul | solution.py:68
  106.3 8.1 %all-to-all-start.1 = ((f32[2,1024,1024]{2,0,1:T(2,128)}), f32[2,1024,1024]{2,0,1:T(2,128)}, u32[]{:S(2)}, u32[]{:S(2)}) async-start(f32[2,1024,1024]{2,0,1:T(2,128)} %copy.129), calls=%async_computation.1 | async-start | bytes 16777216 | tf_op jit(solution)/shard_map/all_to_all | solution.py:70
  115.9 140.9 %all-to-all-done.1 = f32[2,1024,1024]{2,0,1:T(2,128)} async-done(((f32[2,1024,1024]{2,0,1:T(2,128)}), f32[2,1024,1024]{2,0,1:T(2,128)}, u32[]{:S(2)}, u32[]{:S(2)}) %all-to-all-start.1) | async-done | bytes 8388640 | tf_op jit(solution)/shard_map/all_to_all | solution.py:70
  256.8 9.5 %copy.130 = f32[2,1024,1024]{2,1,0:T(8,128)} copy(f32[2,1024,1024]{2,0,1:T(2,128)} %all-to-all-done.1) | data formatting | bytes 16777216 | tf_op jit(solution)/shard_map/all_to_all | solution.py:70
  266.3 7.7 %gather_fusion.5 = f32[32,64,1024]{2,1,0:T(8,128)} fusion(f32[2,16,64,1024]{3,2,1,0:T(8,128)} %bitcast.131, s32[32]{0:T(128)S(1)} %reshape.541), kind=kCustom, calls=%fused_computation.5 | custom fusion | bytes 16777472 | tf_op jit(solution)/shard_map/vmap(jit(_take))/gather | solution.py:13
  274.0 6.0 fusion.1
  280.0 8.7 %copy.131 = f32[2,1024,1024]{2,1,0:T(8,128)} copy(f32[2,1024,1024]{1,2,0:T(8,128)} %fusion.1) | data formatting | bytes 16777216 | tf_op jit(solution)/shard_map/transpose | solution.py:84
  288.7 12.5 %gather_fusion.6 = f32[64,64,1024]{2,1,0:T(8,128)} fusion(f32[2,16,64,1024]{3,2,1,0:T(8,128)} %bitcast.126, s32[64]{0:T(128)S(1)} %reshape.547), kind=kCustom, calls=%fused_computation.6 | custom fusion | bytes 33554944 | tf_op jit(solution)/shard_map/vmap(jit(_take))/gather | solution.py:13
  301.2 7.3 select_multiply_fusion
  308.5 6.7 fusion.77
  315.2 9.7 %bitcast_add_fusion = f32[2048,1024]{1,0:T(8,128)S(1)} fusion(f32[1,32,64,1024]{3,2,1,0:T(8,128)} %get-tuple-element.35, f32[2048,1024]{1,0:T(8,128)} %param.4, f32[1,32,64,1024]{3,2,1,0:T(8,128)} %get-tuple-element.34), kind=kLoop, calls=%fused_computation.10 | loop fusion | flops 4194304 | bytes 33554432 | tf_op jit(solution)/shard_map/add | solution.py:87
  325.0 3.4 copy-done
  328.8 1.3 collective-permute-start
  330.2 8.5 %collective-permute-done = f32[2048,64]{0,1:T(8,128)S(1)} collective-permute-done((f32[2048,64]{0,1:T(8,128)S(1)}, f32[2048,64]{0,1:T(8,128)S(1)}, u32[]{:S(2)}, u32[]{:S(2)}) %collective-permute-start) | collective-permute-done | bytes 524320 | tf_op jit(solution)/shard_map/ppermute | solution.py:91
  338.9 0.9 dynamic-slice_select_fusion.2
  339.8 84.6 %all-gather.3.cloned.1.call-done = f32[16384,64]{1,0:T(8,128)} async-done(((f32[1024,64]{1,0:T(8,128)}), f32[16384,64]{1,0:T(8,128)}) %all-gather.3.cloned.1.call-update) | async-done | bytes 4194320 | tf_op jit(solution)/shard_map/all_gather | solution.py:99
  424.4 8.6 %copy.134 = f32[2,8,1024,64]{2,0,3,1:T(2,128)} copy(f32[2,8,1024,64]{3,2,1,0:T(8,128)} %bitcast.144) | data formatting | bytes 8388608 | tf_op jit(solution)/shard_map/reshape | solution.py:100
  433.0 4.1 copy.143
  437.2 2.0 copy-done.1
  439.3 1.1 stack.2
  440.5 5.7 all-to-all-start.2
  446.6 12.4 %all-to-all-done.2 = f32[8,64,512]{2,1,0:T(8,128)S(1)} async-done(((f32[8,64,512]{2,1,0:T(8,128)}), f32[8,64,512]{2,1,0:T(8,128)S(1)}, u32[]{:S(2)}, u32[]{:S(2)}) %all-to-all-start.2) | async-done | bytes 1048608 | tf_op jit(solution)/shard_map/all_to_all | solution.py:103
  459.6 11.7 %cholesky.104 = f32[128,128]{1,0:T(8,128)S(1)} custom-call(f32[128,128]{1,0:T(8,128)S(1)} %cholesky.266), custom_call_target="Cholesky" | custom-call | tf_op jit(solution)/shard_map/jit(cholesky)/cholesky | solution.py:111
  471.5 9.8 %custom-call.31 = f32[1,128,128]{1,2,0:T(8,128)S(1)} custom-call(f32[1,128,128]{2,1,0:T(8,128)S(1)} %get-tuple-element.45), custom_call_target="InvertDiagBlocksLowerTriangular" | custom-call | tf_op jit(solution)/shard_map/jit(cholesky)/cholesky | solution.py:111
  482.0 11.7 %cholesky.217 = f32[128,128]{1,0:T(8,128)S(1)} custom-call(f32[128,128]{1,0:T(8,128)S(1)} %cholesky.270), custom_call_target="Cholesky" | custom-call | tf_op jit(solution)/shard_map/jit(cholesky)/cholesky | solution.py:111
  494.3 0.7 compare_reduce_fusion.3
  495.1 9.9 %custom-call.32 = f32[1,128,128]{1,2,0:T(8,128)S(1)} custom-call(f32[1,128,128]{2,1,0:T(8,128)S(1)} %get-tuple-element.42), custom_call_target="InvertDiagBlocksLowerTriangular" | custom-call | tf_op jit(solution)/shard_map/jit(cholesky)/cholesky | solution.py:111
  505.7 11.7 %cholesky.238 = f32[128,128]{1,0:T(8,128)S(1)} custom-call(f32[128,128]{1,0:T(8,128)S(1)} %cholesky.275), custom_call_target="Cholesky" | custom-call | tf_op jit(solution)/shard_map/jit(cholesky)/cholesky | solution.py:111
  518.1 9.8 %custom-call.33 = f32[1,128,128]{1,2,0:T(8,128)S(1)} custom-call(f32[1,128,128]{2,1,0:T(8,128)S(1)} %get-tuple-element.39), custom_call_target="InvertDiagBlocksLowerTriangular" | custom-call | tf_op jit(solution)/shard_map/jit(cholesky)/cholesky | solution.py:111
  528.5 11.7 %cholesky.255 = f32[128,128]{1,0:T(8,128)S(1)} custom-call(f32[128,128]{1,0:T(8,128)S(1)} %convolution_subtract_fusion.4), custom_call_target="Cholesky" | custom-call | tf_op jit(solution)/shard_map/jit(cholesky)/cholesky | solution.py:111
  540.2 0.7 compare_reduce_fusion
  544.0 10.5 %while.1 = (s32[]{:T(128)}, f32[512,512]{1,0:T(8,128)S(1)}, s32[4,2]{0,1:T(2,128)S(1)}, f32[4,128,128]{2,1,0:T(8,128)}, s32[]{:T(128)}) while((s32[]{:T(128)}, f32[512,512]{1,0:T(8,128)S(1)}, s32[4,2]{0,1:T(2,128)S(1)}, f32[4,128,128]{2,1,0:T(8,128)}, s32[]{:T(128)}) %tuple.44), condition=%wide.while_cond, body=%wide.while_body.sunk | while | flops 2 | bytes 132705 | solution.py:112
  544.7 2.0 bitcast_dynamic-update-slice_fusion.2
  547.3 2.0 bitcast_dynamic-update-slice_fusion.2
  549.9 2.0 bitcast_dynamic-update-slice_fusion.2
  552.6 2.0 bitcast_dynamic-update-slice_fusion.2
  554.5 40.2 %custom-call.34 = f32[4,128,128]{1,2,0:T(8,128)S(1)} custom-call(f32[4,128,128]{2,1,0:T(8,128)} %get-tuple-element.9), custom_call_target="InvertDiagBlocksLowerTriangular" | custom-call | tf_op jit(solution)/shard_map/jit(_solve_triangular)/triangular_solve | solution.py:112
  594.7 2.4 fusion.15
  597.1 2.2 convolution_subtract_fusion.1
  599.4 1.1 fusion.30
  600.4 2.2 convolution_subtract_fusion
  602.6 1.1 fusion.28
  603.7 3.2 fusion.9
  606.9 1.0 fusion.27
  607.9 1.1 copy-done.5
  609.0 2.4 maximum_bitcast_fusion
  611.4 5.6 copy.140
  617.0 2.8 gather_fusion.2
  619.8 4.2 dynamic-slice_select_fusion
  624.0 6.4 collective-permute-start.1
  630.8 5.5 copy.137
  636.3 5.4 select_select_fusion
  641.6 5.3 copy.141
  647.0 76.4 %collective-permute-done.1 = f32[1024,512]{1,0:T(8,128)} collective-permute-done((f32[1024,512]{1,0:T(8,128)}, f32[1024,512]{1,0:T(8,128)}, u32[]{:S(2)}, u32[]{:S(2)}) %collective-permute-start.1) | collective-permute-done | bytes 2097184 | tf_op jit(solution)/shard_map/ppermute | solution.py:130
  723.4 31.7 %subtract_select_fusion = f32[2048,1024]{1,0:T(8,128)} fusion(f32[2048,1024]{1,0:T(8,128)} %copy-done, pred[1024]{0:T(1024)(128)(4,1)S(1)} %fusion.54, pred[2048]{0:T(1024)(128)(4,1)S(1)} %fusion.48, f32[2048,512]{0,1:T(8,128)} %select_select_fusion, f32[1024,512]{1,0:T(8,128)} %collective-permute-done.1), kind=kOutput, calls=%fused_computation.17 | convolution fusion | flops 12891193344 | bytes 23071744 | tf_op jit(solution)/shard_map/rp,cp->rc/dot_general | solution.py:131
  (121 shorter events, 13.3 us)
Async XLA Ops:
  23.4 52.2 %all-to-all-start = ((f32[2,1024,512]{2,0,1:T(2,128)}), f32[2,1024,512]{2,0,1:T(2,128)}, u32[]{:S(2)}, u32[]{:S(2)}) async-start(f32[2,1024,512]{2,0,1:T(2,128)} %copy.127), calls=%async_computation | async-start | bytes 8388608 | tf_op jit(solution)/shard_map/all_to_all | solution.py:66
  106.3 8.4 %copy-start.7 = (s32[2,128]{1,0:T(2,128)S(1)}, s32[2,128]{1,0:T(2,128)}, u32[]{:S(2)}) copy-start(s32[2,128]{1,0:T(2,128)} %param.6) | copy-start | bytes 3076
  106.3 8.8 %copy-start.8 = (s32[2,128]{1,0:T(2,128)S(1)}, s32[2,128]{1,0:T(2,128)}, u32[]{:S(2)}) copy-start(s32[2,128]{1,0:T(2,128)} %param.7) | copy-start | bytes 3076
  106.3 150.5 %all-to-all-start.1 = ((f32[2,1024,1024]{2,0,1:T(2,128)}), f32[2,1024,1024]{2,0,1:T(2,128)}, u32[]{:S(2)}, u32[]{:S(2)}) async-start(f32[2,1024,1024]{2,0,1:T(2,128)} %copy.129), calls=%async_computation.1 | async-start | bytes 16777216 | tf_op jit(solution)/shard_map/all_to_all | solution.py:70
  114.4 310.0 %all-gather.3.cloned.1.call-start = ((), (), s32[]{:S(2)}) async-start(), calls=%async_computation.3 | async-start | bytes 8912896 | tf_op jit(solution)/shard_map/all_gather | solution.py:99
  325.0 3.4 copy-start
  328.8 9.9 %collective-permute-start = (f32[2048,64]{0,1:T(8,128)S(1)}, f32[2048,64]{0,1:T(8,128)S(1)}, u32[]{:S(2)}, u32[]{:S(2)}) collective-permute-start(f32[2048,64]{0,1:T(8,128)S(1)} %copy.132), channel_id=1, source_target_pairs={{0,8},{1,9},{2,10},{3,11},{4,12},{5,13},{6,14},{7,15},{16,24},{17,... | collective-permute-start | bytes 1572872 | tf_op jit(solution)/shard_map/ppermute | solution.py:91
  437.2 2.0 copy-start.1
  440.5 18.5 %all-to-all-start.2 = ((f32[8,64,512]{2,1,0:T(8,128)}), f32[8,64,512]{2,1,0:T(8,128)S(1)}, u32[]{:S(2)}, u32[]{:S(2)}) async-start(f32[8,64,512]{2,1,0:T(8,128)} %stack.2), calls=%async_computation.2 | async-start | bytes 2097152 | tf_op jit(solution)/shard_map/all_to_all | solution.py:103
  554.5 42.6 %copy-start.6 = (f32[512,512]{1,0:T(8,128)}, f32[512,512]{1,0:T(8,128)S(1)}, u32[]{:S(2)}) copy-start(f32[512,512]{1,0:T(8,128)S(1)} %get-tuple-element.111) | copy-start | bytes 3145732
  594.7 5.7 copy-start.2
  603.7 4.2 copy-start.3
  607.9 1.1 copy-start.5
  624.0 99.3 %collective-permute-start.1 = (f32[1024,512]{1,0:T(8,128)}, f32[1024,512]{1,0:T(8,128)}, u32[]{:S(2)}, u32[]{:S(2)}) collective-permute-start(f32[1024,512]{1,0:T(8,128)} %bitcast.41), channel_id=1, source_target_pairs={{0,0},{1,16},{2,32},{3,48},{4,64},{5,80},{6,96},{7,112},{8,8},{9,2... | collective-permute-start | bytes 6291464 | tf_op jit(solution)/shard_map/ppermute | solution.py:130
  630.8 5.5 copy-start.4
Sparse Core Ops, SparseCore 0:
  339.9 84.4 all-gather.2
